TPU v7x, 512 devices: a whole 4x8x8 slice. The times are simulated.
512 devices in a mesh: chan: 32 (over y_hi, x, core), tm: 16 (over y_lo, z).
Axes of the slice: x: 4, y: 8 (y_hi: 4, y_lo: 2; y = y_hi * 2 + y_lo), z: 8, core: 2. Of those that a mesh axis runs over, the one named last changes fastest.
Arguments:
- raw_strain: float32 [2048, 16384], P('chan', 'tm'), may hold values from -2000 to 2000
- fir_taps: float32 [64], replicated, may hold values from -0.75 to 0.75
- block_mask: int32 [32, 32], replicated, may hold values 0 or 1
Outputs:
- correlations: float32 [128, 2048, 2048], P('tm', 'chan')
All inputs are finite; a program needn't handle non-finite values.
Results may differ from a plain program's by a relative error of at most 0.0054.
Values may be sent and summed in bfloat16 or wider, within the bound.
No kernel may reach another device: no remote copies, remote signals or barrier semaphores. Data moves between devices by JAX's collectives and lax.ppermute only.
A program may use at most 64 MiB of HBM per device.

v0:
```python
import math
import jax
import jax.numpy as jnp
from jax import lax
from jax.sharding import PartitionSpec as P

DECIM = 8
TAPS = 64
LAGS = 128


def from_behind(value, axis, steps):
    count = lax.axis_size(axis)
    first, last = (max(0, -steps), min(count, count - steps))
    return lax.ppermute(value, axis, [(source, source + steps) for source in range(first, last)])


def decimate(raw_strain, fir_taps):
    time_span = raw_strain.shape[1]
    margin = TAPS - DECIM
    earlier = from_behind(raw_strain[:, time_span - margin :], "tm", 1)
    extended = jnp.concatenate([earlier, raw_strain], axis=1)
    outputs = time_span // DECIM
    tap_blocks = TAPS // DECIM
    frames = outputs + tap_blocks - 1
    tap_table = fir_taps[::-1].reshape(tap_blocks, DECIM)
    shape_three = (frames, outputs, tap_blocks)
    matches = lax.broadcasted_iota(jnp.int32, shape_three, 0) - lax.broadcasted_iota(
        jnp.int32, shape_three, 1
    ) == lax.broadcasted_iota(jnp.int32, shape_three, 2)
    one_hot = matches.astype(jnp.float32)
    filter_matrix = jnp.einsum("mtj,jr->mrt", one_hot, tap_table, precision=lax.Precision.HIGHEST)
    filter_matrix = filter_matrix.reshape(frames * DECIM, outputs)
    return jnp.dot(
        extended, filter_matrix, precision=lax.Precision.HIGHEST, preferred_element_type=jnp.float32
    )


def per_device(raw_strain, fir_taps, block_mask):
    channel_rows = raw_strain.shape[0]
    decimated = decimate(raw_strain, fir_taps)
    rounded = decimated.astype(jnp.bfloat16)
    time_span = rounded.shape[1]
    tm_parts = lax.axis_size("tm")
    samples = time_span * tm_parts
    gathered = lax.all_gather(rounded, "tm", axis=1, tiled=True)
    full_values = gathered.astype(jnp.float32)
    root_whole = jnp.sqrt(jnp.mean(full_values * full_values, axis=1, keepdims=True) + 1e-06)
    caches = (full_values / root_whole).astype(jnp.bfloat16)
    lag_count = LAGS // tm_parts
    tm_index = lax.axis_index("tm")
    lag_base = tm_index * lag_count
    anchor = jnp.zeros((), jnp.int32)
    initial = jnp.zeros(
        (lag_count, channel_rows, channel_rows * lax.axis_size("chan")), jnp.float32
    )
    shard_piece = lax.all_gather(caches, "chan", axis=0, tiled=True)
    first_index = jnp.int32(0)
    piece_width = shard_piece.shape[0]
    padded_piece = jnp.pad(shard_piece, ((0, 0), (0, LAGS)))

    def one_lag(lag_step, running):
        shifted = lax.dynamic_slice_in_dim(padded_piece, lag_base + lag_step, samples, 1)
        product = lax.dot_general(
            caches, shifted, (((1,), (1,)), ((), ())), preferred_element_type=jnp.float32
        )
        where_at = (lag_step, anchor, first_index)
        current = lax.dynamic_slice(running, where_at, (1, channel_rows, piece_width))
        return lax.dynamic_update_slice(running, current + product[None], where_at)

    correlated = lax.fori_loop(0, lag_count, one_lag, initial)
    mask_row = lax.dynamic_index_in_dim(block_mask, lax.axis_index("chan"), 0, keepdims=False)
    weights = jnp.repeat(mask_row, channel_rows).astype(jnp.float32) * (1.0 / math.sqrt(samples))
    return correlated * weights[None, None, :]


def solution(mesh):
    placed = (P("chan", "tm"), P(), P())
    return jax.shard_map(
        per_device, mesh=mesh, in_specs=placed, out_specs=P("tm", "chan", None), check_vma=False
    )
```

profile of v0, /device:TPU:17, one launch (start us, length us, event | category | flops | bytes accessed | tf_op | source)
XLA Modules:
  0.0 219.1 jit_solution(5011104009306333967)
XLA Ops:
  6.5 0.0 all-gather.2.cloned.1.call-start
  6.5 0.8 slice.3
  7.4 4.0 %collective-permute-start = (f32[64,56]{1,0:T(8,128)S(1)}, f32[64,56]{1,0:T(8,128)S(1)}, u32[]{:S(2)}, u32[]{:S(2)}) collective-permute-start(f32[64,56]{1,0:T(8,128)S(1)} %slice.3), channel_id=1, source_target_pairs={{0,1},{1,2},{2,3},{3,4},{4,5},{5,6},{6,7},{7,8},{8,9},{9,10},{10,1... | collective-permute-start | bytes 43016 | tf_op jit(solution)/shard_map/ppermute | solution.py:15
  11.4 0.7 rev.3
  12.1 0.1 reshape.27
  12.2 0.4 convolution_bitcast_fusion
  12.6 0.0 collective-permute-done
  12.7 1.5 convolution_convert_fusion
  14.1 33.4 %all_gather.6 = bf16[64,2048]{1,0:T(8,128)(2,1)S(1)} all-gather(bf16[64,128]{1,0:T(8,128)(2,1)S(1)} %convolution_convert_fusion), channel_id=1, replica_groups=mesh['chan'=32,'tm'=16] {'tm'}, dimensions={1}, use_global_device_ids=true | all-gather | bytes 278528 | tf_op jit(solution)/shard_map/all_gather | solution.py:46
  47.5 0.2 fusion.12
  47.7 0.8 fusion.13
  48.5 0.0 all-gather.2.cloned.1.call-update
  48.6 0.7 multiply_bitcast_fusion
  49.3 0.1 broadcast_in_dim.16
  49.3 0.1 mul.36
  49.4 86.4 %all-gather.2.cloned.1.call-done = bf16[2048,2048]{1,0:T(8,128)(2,1)} async-done(((bf16[64,2048]{1,0:T(8,128)(2,1)}), bf16[2048,2048]{1,0:T(8,128)(2,1)}) %all-gather.2.cloned.1.call-update) | async-done | bytes 8388624 | tf_op jit(solution)/shard_map/all_gather | solution.py:57
  135.8 7.8 %pad.4 = bf16[2048,2176]{1,0:T(8,128)(2,1)} pad(bf16[2048,2048]{1,0:T(8,128)(2,1)} %all-gather.2.cloned.1.call-done, bf16[]{:T(256)} %constant.53.clone.1), padding=0_0x0_128 | pad | bytes 17301506 | tf_op jit(solution)/shard_map/jit(_pad)/pad | solution.py:60
  143.6 0.0 copy-start
  143.6 2.5 %broadcast_in_dim.15 = f32[8,64,2048]{2,1,0:T(8,128)} broadcast(f32[]{:T(128)} %constant.48.clone.1), dimensions={} | broadcast | bytes 4194308 | tf_op jit(solution)/shard_map/broadcast_in_dim | solution.py:54
  146.1 0.0 copy-done
  146.1 61.2 %while.13 = (s32[]{:T(128)}, f32[8,64,2048]{2,1,0:T(8,128)}, s32[]{:T(128)}, bf16[2048,2176]{1,0:T(8,128)(2,1)}, bf16[64,2048]{1,0:T(8,128)(2,1)S(1)}, /*index=5*/s32[]{:T(128)}, s32[]{:T(128)}, s32[]{:T(128)}) while((s32[]{:T(128)}, f32[8,64,2048]{2,1,0:T(8,128)}, s32[]{:T(128)}, bf16[2048,2176]{1,0:T(8,128)(2,1)}, ...), condition=%wide.region_2.3_spmd, body=%wide.region_1.2_spmd.sunk | while | flops 537001984 | bytes 9699475 | solution.py:71
  146.1 7.7 %fusion.26 = f32[8,64,2048]{2,1,0:T(8,128)} fusion(f32[8,64,2048]{2,1,0:T(8,128)} %get-tuple-element.150, s32[]{:T(128)S(6)} %copy.10, bf16[64,2048]{1,0:T(8,128)(2,1)S(1)} %get-tuple-element.161, bf16[2048,2176]{1,0:T(8,128)(2,1)} %get-tuple-element.160, s32[]{:T(128)S(6)} %select_n.19), kind=kOutput, calls=%fused_computation.4.clone.1 | convolution fusion | flops 537001984 | bytes 9699336 | tf_op jit(solution)/shard_map/while/body/eval_jaxpr/dot_general | solution.py:64
  153.8 7.7 %fusion.26 = f32[8,64,2048]{2,1,0:T(8,128)} fusion(f32[8,64,2048]{2,1,0:T(8,128)} %get-tuple-element.150, s32[]{:T(128)S(6)} %copy.10, bf16[64,2048]{1,0:T(8,128)(2,1)S(1)} %get-tuple-element.161, bf16[2048,2176]{1,0:T(8,128)(2,1)} %get-tuple-element.160, s32[]{:T(128)S(6)} %select_n.19), kind=kOutput, calls=%fused_computation.4.clone.1 | convolution fusion | flops 537001984 | bytes 9699336 | tf_op jit(solution)/shard_map/while/body/eval_jaxpr/dot_general | solution.py:64
  161.4 7.7 %fusion.26 = f32[8,64,2048]{2,1,0:T(8,128)} fusion(f32[8,64,2048]{2,1,0:T(8,128)} %get-tuple-element.150, s32[]{:T(128)S(6)} %copy.10, bf16[64,2048]{1,0:T(8,128)(2,1)S(1)} %get-tuple-element.161, bf16[2048,2176]{1,0:T(8,128)(2,1)} %get-tuple-element.160, s32[]{:T(128)S(6)} %select_n.19), kind=kOutput, calls=%fused_computation.4.clone.1 | convolution fusion | flops 537001984 | bytes 9699336 | tf_op jit(solution)/shard_map/while/body/eval_jaxpr/dot_general | solution.py:64
  169.1 7.7 %fusion.26 = f32[8,64,2048]{2,1,0:T(8,128)} fusion(f32[8,64,2048]{2,1,0:T(8,128)} %get-tuple-element.150, s32[]{:T(128)S(6)} %copy.10, bf16[64,2048]{1,0:T(8,128)(2,1)S(1)} %get-tuple-element.161, bf16[2048,2176]{1,0:T(8,128)(2,1)} %get-tuple-element.160, s32[]{:T(128)S(6)} %select_n.19), kind=kOutput, calls=%fused_computation.4.clone.1 | convolution fusion | flops 537001984 | bytes 9699336 | tf_op jit(solution)/shard_map/while/body/eval_jaxpr/dot_general | solution.py:64
  176.8 7.7 %fusion.26 = f32[8,64,2048]{2,1,0:T(8,128)} fusion(f32[8,64,2048]{2,1,0:T(8,128)} %get-tuple-element.150, s32[]{:T(128)S(6)} %copy.10, bf16[64,2048]{1,0:T(8,128)(2,1)S(1)} %get-tuple-element.161, bf16[2048,2176]{1,0:T(8,128)(2,1)} %get-tuple-element.160, s32[]{:T(128)S(6)} %select_n.19), kind=kOutput, calls=%fused_computation.4.clone.1 | convolution fusion | flops 537001984 | bytes 9699336 | tf_op jit(solution)/shard_map/while/body/eval_jaxpr/dot_general | solution.py:64
  184.4 7.7 %fusion.26 = f32[8,64,2048]{2,1,0:T(8,128)} fusion(f32[8,64,2048]{2,1,0:T(8,128)} %get-tuple-element.150, s32[]{:T(128)S(6)} %copy.10, bf16[64,2048]{1,0:T(8,128)(2,1)S(1)} %get-tuple-element.161, bf16[2048,2176]{1,0:T(8,128)(2,1)} %get-tuple-element.160, s32[]{:T(128)S(6)} %select_n.19), kind=kOutput, calls=%fused_computation.4.clone.1 | convolution fusion | flops 537001984 | bytes 9699336 | tf_op jit(solution)/shard_map/while/body/eval_jaxpr/dot_general | solution.py:64
  192.1 7.7 %fusion.26 = f32[8,64,2048]{2,1,0:T(8,128)} fusion(f32[8,64,2048]{2,1,0:T(8,128)} %get-tuple-element.150, s32[]{:T(128)S(6)} %copy.10, bf16[64,2048]{1,0:T(8,128)(2,1)S(1)} %get-tuple-element.161, bf16[2048,2176]{1,0:T(8,128)(2,1)} %get-tuple-element.160, s32[]{:T(128)S(6)} %select_n.19), kind=kOutput, calls=%fused_computation.4.clone.1 | convolution fusion | flops 537001984 | bytes 9699336 | tf_op jit(solution)/shard_map/while/body/eval_jaxpr/dot_general | solution.py:64
  199.7 7.7 %fusion.26 = f32[8,64,2048]{2,1,0:T(8,128)} fusion(f32[8,64,2048]{2,1,0:T(8,128)} %get-tuple-element.150, s32[]{:T(128)S(6)} %copy.10, bf16[64,2048]{1,0:T(8,128)(2,1)S(1)} %get-tuple-element.161, bf16[2048,2176]{1,0:T(8,128)(2,1)} %get-tuple-element.160, s32[]{:T(128)S(6)} %select_n.19), kind=kOutput, calls=%fused_computation.4.clone.1 | convolution fusion | flops 537001984 | bytes 9699336 | tf_op jit(solution)/shard_map/while/body/eval_jaxpr/dot_general | solution.py:64
  207.4 4.9 %broadcast_multiply_fusion = f32[8,64,2048]{2,1,0:T(8,128)} fusion(f32[8,64,2048]{2,1,0:T(8,128)} %get-tuple-element.99, f32[2048]{0:T(1024)S(1)} %mul.36), kind=kLoop, calls=%fused_computation.7 | loop fusion | flops 1048576 | bytes 8396800 | tf_op jit(solution)/shard_map/mul | solution.py:74
  (1 shorter events, 0.0 us)
Async XLA Ops:
  6.5 129.2 %all-gather.2.cloned.1.call-start = ((), (), s32[]{:S(2)}) async-start(), calls=%async_computation | async-start | bytes 8650752 | tf_op jit(solution)/shard_map/all_gather | solution.py:57
  7.4 5.3 %collective-permute-start = (f32[64,56]{1,0:T(8,128)S(1)}, f32[64,56]{1,0:T(8,128)S(1)}, u32[]{:S(2)}, u32[]{:S(2)}) collective-permute-start(f32[64,56]{1,0:T(8,128)S(1)} %slice.3), channel_id=1, source_target_pairs={{0,1},{1,2},{2,3},{3,4},{4,5},{5,6},{6,7},{7,8},{8,9},{9,10},{10,1... | collective-permute-start | bytes 43016 | tf_op jit(solution)/shard_map/ppermute | solution.py:15
  143.6 2.5 %copy-start = (bf16[64,2048]{1,0:T(8,128)(2,1)S(1)}, bf16[64,2048]{1,0:T(8,128)(2,1)}, u32[]{:S(2)}) copy-start(bf16[64,2048]{1,0:T(8,128)(2,1)} %fusion.13) | copy-start | bytes 786436
Sparse Core Ops, SparseCore 0:
  48.7 87.0 all-gather.1
where the time goes:
time: 219 us
  waiting for transfers between devices  86.4 us (39%)
  matrix products  63.1 us (29%)
  blocking collectives  33.4 us (15%)
  between operations  13.4 us (6%)
  local copies, waits for them, and re-layouts  12.1 us (6%)
  other arithmetic  6.58 us (3%)
  starting transfers between devices  3.99 us (2%)
    all_gather x1, waiting for transfers between devices, per_device(): shard_piece = lax.all_gather(caches, 'chan', axis=0, tiled=True)  86.4 us
    dot_general x8, matrix products, one_lag(): lax.dot_general(caches, shifted, (((1,), (1,)), ((), ())), preferred_elem...  61.2 us
    all_gather x1, blocking collectives, per_device(): gathered = lax.all_gather(rounded, 'tm', axis=1, tiled=True)  33.4 us
    pad x1, local copies, waits for them, and re-layouts, per_device(): padded_piece = jnp.pad(shard_piece, ((0, 0), (0, LAGS)))  7.82 us
    mul x1, other arithmetic, per_device(): return correlated * weights[None, None, :]  4.89 us
  transfers between devices with their start and end apart: 2, of which 1 were waited for; matrix products, arithmetic and copies ran while one was open for 1% of the time, Pallas kernels for 0%

commit v1 on v0

--- a/solution.py
+++ b/solution.py
@@ -43,7 +43,9 @@
     time_span = rounded.shape[1]
     tm_parts = lax.axis_size("tm")
     samples = time_span * tm_parts
-    gathered = lax.all_gather(rounded, "tm", axis=1, tiled=True)
+    gathered = jnp.concatenate(
+        lax.all_to_all(jnp.stack([rounded] * lax.axis_size("tm")), "tm", 0, 0), axis=1
+    )
     full_values = gathered.astype(jnp.float32)
     root_whole = jnp.sqrt(jnp.mean(full_values * full_values, axis=1, keepdims=True) + 1e-06)
     caches = (full_values / root_whole).astype(jnp.bfloat16)

time: 219 us -> 201 us (0.918)
  blocking collectives: 33.4 us -> 19.2 us
  waiting for transfers between devices: 86.4 us -> 82.6 us
    all_gather x1 -> x0, blocking collectives: 33.4 us -> none  [per_device(): gathered = lax.all_gather(rounded, 'tm', axis=1, tiled=True)]
    all_to_all x0 -> x1, blocking collectives: none -> 19.2 us  [per_device(): lax.all_to_all(jnp.stack([rounded] * lax.axis_size('tm')), 'tm', 0, 0)]
    all_gather x1, waiting for transfers between devices: 86.4 us -> 82.6 us  [per_device(): shard_piece = lax.all_gather(caches, 'chan', axis=0, tiled=True)]
where the time goes in v1:
time: 201 us
  waiting for transfers between devices  82.6 us (41%)
  matrix products  63.1 us (31%)
  blocking collectives  19.2 us (10%)
  between operations  13.4 us (7%)
  local copies, waits for them, and re-layouts  12.2 us (6%)
  other arithmetic  6.58 us (3%)
  starting transfers between devices  3.99 us (2%)
    all_gather x1, waiting for transfers between devices, per_device(): shard_piece = lax.all_gather(caches, 'chan', axis=0, tiled=True)  82.6 us
    dot_general x8, matrix products, one_lag(): lax.dot_general(caches, shifted, (((1,), (1,)), ((), ())), preferred_elem...  61.2 us
    all_to_all x1, blocking collectives, per_device(): lax.all_to_all(jnp.stack([rounded] * lax.axis_size('tm')), 'tm', 0, 0)  19.2 us
    pad x1, local copies, waits for them, and re-layouts, per_device(): padded_piece = jnp.pad(shard_piece, ((0, 0), (0, LAGS)))  7.82 us
    mul x1, other arithmetic, per_device(): return correlated * weights[None, None, :]  4.89 us
  transfers between devices with their start and end apart: 2, of which 1 were waited for; matrix products, arithmetic and copies ran while one was open for 1% of the time, Pallas kernels for 0%

profile of v1, /device:TPU:17, one launch (start us, length us, event | category | flops | bytes accessed | tf_op | source)
XLA Modules:
  0.0 201.1 jit_solution(12012675638693323368)
XLA Ops:
  6.5 0.0 all-gather.2.cloned.1.call-start
  6.5 0.8 slice.3
  7.4 4.0 %collective-permute-start = (f32[64,56]{1,0:T(8,128)S(1)}, f32[64,56]{1,0:T(8,128)S(1)}, u32[]{:S(2)}, u32[]{:S(2)}) collective-permute-start(f32[64,56]{1,0:T(8,128)S(1)} %slice.3), channel_id=1, source_target_pairs={{0,1},{1,2},{2,3},{3,4},{4,5},{5,6},{6,7},{7,8},{8,9},{9,10},{10,1... | collective-permute-start | bytes 43016 | tf_op jit(solution)/shard_map/ppermute | solution.py:15
  11.4 0.7 rev.3
  12.1 0.1 reshape.33
  12.2 0.4 convolution_bitcast_fusion
  12.6 0.0 collective-permute-done
  12.7 1.5 convolution_convert_fusion
  14.2 19.2 %all_to_all.5 = bf16[16,64,128]{2,1,0:T(8,128)(2,1)S(1)} all-to-all(bf16[16,64,128]{2,1,0:T(8,128)(2,1)S(1)} %stack.2), channel_id=1, replica_groups=mesh['chan'=32,'tm'=16] {'tm'}, dimensions={0} | all-to-all | bytes 524288 | tf_op jit(solution)/shard_map/all_to_all | solution.py:47
  33.3 0.2 fusion.12
  33.5 0.8 fusion.13
  34.3 0.0 all-gather.2.cloned.1.call-update
  34.4 0.7 multiply_bitcast_fusion
  35.1 0.1 broadcast_in_dim.16
  35.1 0.1 mul.38
  35.2 82.6 %all-gather.2.cloned.1.call-done = bf16[2048,2048]{1,0:T(8,128)(2,1)} async-done(((bf16[64,2048]{1,0:T(8,128)(2,1)}), bf16[2048,2048]{1,0:T(8,128)(2,1)}) %all-gather.2.cloned.1.call-update) | async-done | bytes 8388624 | tf_op jit(solution)/shard_map/all_gather | solution.py:59
  117.8 7.8 %pad.4 = bf16[2048,2176]{1,0:T(8,128)(2,1)} pad(bf16[2048,2048]{1,0:T(8,128)(2,1)} %all-gather.2.cloned.1.call-done, bf16[]{:T(256)} %constant.53.clone.1), padding=0_0x0_128 | pad | bytes 17301506 | tf_op jit(solution)/shard_map/jit(_pad)/pad | solution.py:62
  125.6 0.0 copy-start
  125.6 2.5 %broadcast_in_dim.15 = f32[8,64,2048]{2,1,0:T(8,128)} broadcast(f32[]{:T(128)} %constant.48.clone.1), dimensions={} | broadcast | bytes 4194308 | tf_op jit(solution)/shard_map/broadcast_in_dim | solution.py:56
  128.2 0.0 copy-done
  128.2 61.2 %while.13 = (s32[]{:T(128)}, f32[8,64,2048]{2,1,0:T(8,128)}, s32[]{:T(128)}, bf16[2048,2176]{1,0:T(8,128)(2,1)}, bf16[64,2048]{1,0:T(8,128)(2,1)S(1)}, /*index=5*/s32[]{:T(128)}, s32[]{:T(128)}, s32[]{:T(128)}) while((s32[]{:T(128)}, f32[8,64,2048]{2,1,0:T(8,128)}, s32[]{:T(128)}, bf16[2048,2176]{1,0:T(8,128)(2,1)}, ...), condition=%wide.region_2.3_spmd, body=%wide.region_1.2_spmd.sunk | while | flops 537001984 | bytes 9699475 | solution.py:73
  128.2 7.7 %fusion.26 = f32[8,64,2048]{2,1,0:T(8,128)} fusion(f32[8,64,2048]{2,1,0:T(8,128)} %get-tuple-element.150, s32[]{:T(128)S(6)} %copy.15, bf16[64,2048]{1,0:T(8,128)(2,1)S(1)} %get-tuple-element.161, bf16[2048,2176]{1,0:T(8,128)(2,1)} %get-tuple-element.160, s32[]{:T(128)S(6)} %select_n.19), kind=kOutput, calls=%fused_computation.4.clone.1 | convolution fusion | flops 537001984 | bytes 9699336 | tf_op jit(solution)/shard_map/while/body/eval_jaxpr/dot_general | solution.py:66
  135.8 7.7 %fusion.26 = f32[8,64,2048]{2,1,0:T(8,128)} fusion(f32[8,64,2048]{2,1,0:T(8,128)} %get-tuple-element.150, s32[]{:T(128)S(6)} %copy.15, bf16[64,2048]{1,0:T(8,128)(2,1)S(1)} %get-tuple-element.161, bf16[2048,2176]{1,0:T(8,128)(2,1)} %get-tuple-element.160, s32[]{:T(128)S(6)} %select_n.19), kind=kOutput, calls=%fused_computation.4.clone.1 | convolution fusion | flops 537001984 | bytes 9699336 | tf_op jit(solution)/shard_map/while/body/eval_jaxpr/dot_general | solution.py:66
  143.5 7.7 %fusion.26 = f32[8,64,2048]{2,1,0:T(8,128)} fusion(f32[8,64,2048]{2,1,0:T(8,128)} %get-tuple-element.150, s32[]{:T(128)S(6)} %copy.15, bf16[64,2048]{1,0:T(8,128)(2,1)S(1)} %get-tuple-element.161, bf16[2048,2176]{1,0:T(8,128)(2,1)} %get-tuple-element.160, s32[]{:T(128)S(6)} %select_n.19), kind=kOutput, calls=%fused_computation.4.clone.1 | convolution fusion | flops 537001984 | bytes 9699336 | tf_op jit(solution)/shard_map/while/body/eval_jaxpr/dot_general | solution.py:66
  151.1 7.7 %fusion.26 = f32[8,64,2048]{2,1,0:T(8,128)} fusion(f32[8,64,2048]{2,1,0:T(8,128)} %get-tuple-element.150, s32[]{:T(128)S(6)} %copy.15, bf16[64,2048]{1,0:T(8,128)(2,1)S(1)} %get-tuple-element.161, bf16[2048,2176]{1,0:T(8,128)(2,1)} %get-tuple-element.160, s32[]{:T(128)S(6)} %select_n.19), kind=kOutput, calls=%fused_computation.4.clone.1 | convolution fusion | flops 537001984 | bytes 9699336 | tf_op jit(solution)/shard_map/while/body/eval_jaxpr/dot_general | solution.py:66
  158.8 7.7 %fusion.26 = f32[8,64,2048]{2,1,0:T(8,128)} fusion(f32[8,64,2048]{2,1,0:T(8,128)} %get-tuple-element.150, s32[]{:T(128)S(6)} %copy.15, bf16[64,2048]{1,0:T(8,128)(2,1)S(1)} %get-tuple-element.161, bf16[2048,2176]{1,0:T(8,128)(2,1)} %get-tuple-element.160, s32[]{:T(128)S(6)} %select_n.19), kind=kOutput, calls=%fused_computation.4.clone.1 | convolution fusion | flops 537001984 | bytes 9699336 | tf_op jit(solution)/shard_map/while/body/eval_jaxpr/dot_general | solution.py:66
  166.4 7.7 %fusion.26 = f32[8,64,2048]{2,1,0:T(8,128)} fusion(f32[8,64,2048]{2,1,0:T(8,128)} %get-tuple-element.150, s32[]{:T(128)S(6)} %copy.15, bf16[64,2048]{1,0:T(8,128)(2,1)S(1)} %get-tuple-element.161, bf16[2048,2176]{1,0:T(8,128)(2,1)} %get-tuple-element.160, s32[]{:T(128)S(6)} %select_n.19), kind=kOutput, calls=%fused_computation.4.clone.1 | convolution fusion | flops 537001984 | bytes 9699336 | tf_op jit(solution)/shard_map/while/body/eval_jaxpr/dot_general | solution.py:66
  174.1 7.7 %fusion.26 = f32[8,64,2048]{2,1,0:T(8,128)} fusion(f32[8,64,2048]{2,1,0:T(8,128)} %get-tuple-element.150, s32[]{:T(128)S(6)} %copy.15, bf16[64,2048]{1,0:T(8,128)(2,1)S(1)} %get-tuple-element.161, bf16[2048,2176]{1,0:T(8,128)(2,1)} %get-tuple-element.160, s32[]{:T(128)S(6)} %select_n.19), kind=kOutput, calls=%fused_computation.4.clone.1 | convolution fusion | flops 537001984 | bytes 9699336 | tf_op jit(solution)/shard_map/while/body/eval_jaxpr/dot_general | solution.py:66
  181.7 7.7 %fusion.26 = f32[8,64,2048]{2,1,0:T(8,128)} fusion(f32[8,64,2048]{2,1,0:T(8,128)} %get-tuple-element.150, s32[]{:T(128)S(6)} %copy.15, bf16[64,2048]{1,0:T(8,128)(2,1)S(1)} %get-tuple-element.161, bf16[2048,2176]{1,0:T(8,128)(2,1)} %get-tuple-element.160, s32[]{:T(128)S(6)} %select_n.19), kind=kOutput, calls=%fused_computation.4.clone.1 | convolution fusion | flops 537001984 | bytes 9699336 | tf_op jit(solution)/shard_map/while/body/eval_jaxpr/dot_general | solution.py:66
  189.4 4.9 %broadcast_multiply_fusion = f32[8,64,2048]{2,1,0:T(8,128)} fusion(f32[8,64,2048]{2,1,0:T(8,128)} %get-tuple-element.99, f32[2048]{0:T(1024)S(1)} %mul.38), kind=kLoop, calls=%fused_computation.7 | loop fusion | flops 1048576 | bytes 8396800 | tf_op jit(solution)/shard_map/mul | solution.py:76
  (2 shorter events, 0.1 us)
Async XLA Ops:
  6.5 111.3 %all-gather.2.cloned.1.call-start = ((), (), s32[]{:S(2)}) async-start(), calls=%async_computation.1 | async-start | bytes 8650752 | tf_op jit(solution)/shard_map/all_gather | solution.py:59
  7.4 5.3 %collective-permute-start = (f32[64,56]{1,0:T(8,128)S(1)}, f32[64,56]{1,0:T(8,128)S(1)}, u32[]{:S(2)}, u32[]{:S(2)}) collective-permute-start(f32[64,56]{1,0:T(8,128)S(1)} %slice.3), channel_id=1, source_target_pairs={{0,1},{1,2},{2,3},{3,4},{4,5},{5,6},{6,7},{7,8},{8,9},{9,10},{10,1... | collective-permute-start | bytes 43016 | tf_op jit(solution)/shard_map/ppermute | solution.py:15
  125.6 2.5 %copy-start = (bf16[64,2048]{1,0:T(8,128)(2,1)S(1)}, bf16[64,2048]{1,0:T(8,128)(2,1)}, u32[]{:S(2)}) copy-start(bf16[64,2048]{1,0:T(8,128)(2,1)} %fusion.13) | copy-start | bytes 786436
Sparse Core Ops, SparseCore 0:
  34.5 83.2 all-gather.1
